TPU v7x, 512 devices: a whole 4x4x16 slice. The times are simulated.
512 devices in a mesh: tensor: 32 (over z_hi, x, core), seq: 16 (over z_lo, y).
Axes of the slice: x: 4, y: 4, z: 16 (z_hi: 4, z_lo: 4; z = z_hi * 4 + z_lo), core: 2. Of those that a mesh axis runs over, the one named last changes fastest.
Arguments:
- resid: bfloat16 [16, 512, 2048], P('seq', 'tensor'), may hold values from -6 to 6
- norm_gain: bfloat16 [2048], replicated, may hold values from 0.099609375 to 1.8984375
- gate_weight_matrix: bfloat16 [2048, 10944], P(None, 'tensor'), may hold values from -0.125 to 0.125
- up_weight: bfloat16 [2048, 10944], P(None, 'tensor'), may hold values from -0.125 to 0.125
- w_down: bfloat16 [10944, 2048], P('tensor'), may hold values from -0.0546875 to 0.0546875
- gate_a: bfloat16 [64, 2048, 16], P('seq', 'tensor'), may hold values from -0.125 to 0.125
- gate_b: bfloat16 [64, 16, 10944], P('seq', None, 'tensor'), may hold values from -1.5 to 1.5
- up_a: bfloat16 [64, 2048, 16], P('seq', 'tensor'), may hold values from -0.125 to 0.125
- up_b: bfloat16 [64, 16, 10944], P('seq', None, 'tensor'), may hold values from -1.5 to 1.5
- down_a: bfloat16 [64, 10944, 16], P('seq', 'tensor'), may hold values from -0.0546875 to 0.0546875
- down_b: bfloat16 [64, 16, 2048], P('seq'), may hold values from -1.5 to 1.5
- prompt_lengths: int32 [16, 8], P('seq'), may hold values from 1 to 256, 512 in all within a row
- prompt_choice: int32 [16, 8], P('seq'), may hold values from 0 to 15
- used_adapters: int32 [16], replicated, may hold values from 0 to 63, as said below
- adapter_holder: int32 [64], replicated, may hold values from 0 to 63, each once
Outputs:
- output: bfloat16 [16, 512, 2048], P('seq', 'tensor')
Inputs may be any that keep to these rules, and one draw needn't show every extreme that they name: `used_adapters`: 16 distinct adapter ids.
All inputs are finite; a program needn't handle non-finite values.
Results may differ from a plain program's by a relative error of at most 0.017.
Values may be sent and summed in bfloat16 or wider, within the bound.
No kernel may reach another device: no remote copies, remote signals or barrier semaphores. Data moves between devices by JAX's collectives and lax.ppermute only.
A program may use at most 128 MiB of HBM per device.

v0:
```python
import jax
import jax.numpy as jnp
from jax import lax
from jax.sharding import PartitionSpec as P

adapter_scale = 0.5


def choose(picker, stacked):
    flat = stacked.reshape(stacked.shape[0], -1)
    chosen = jnp.dot(picker, flat, preferred_element_type=jnp.float32).astype(jnp.bfloat16)
    return chosen.reshape((picker.shape[0],) + stacked.shape[1:])


def to_columns(stacked):
    used_n, inner, rank_n = stacked.shape
    return jnp.transpose(stacked, (1, 0, 2)).reshape(inner, used_n * rank_n)


def local(
    resid,
    norm_gain,
    gate_weight_matrix,
    up_weight,
    w_down,
    gate_a,
    gate_b,
    up_a,
    up_b,
    down_a,
    down_b,
    prompt_lengths,
    prompt_choice,
    used_adapters,
    adapter_holder,
):
    tensor_n = lax.axis_size("tensor")
    tok_dev = resid.shape[1]
    group_tok = tok_dev * tensor_n
    used_n = used_adapters.shape[0]
    rank_n = gate_a.shape[2]
    feat_loc = gate_a.shape[1]
    hidden_local = gate_weight_matrix.shape[1]
    adapters_n = adapter_holder.shape[0]
    matches = used_adapters[:, None] == jnp.arange(adapters_n, dtype=jnp.int32)[None, :]
    slot_used = jnp.sum(jnp.where(matches, adapter_holder[None, :], 0), axis=1)
    whole = (
        lax.all_gather(gate_a, "seq", axis=0, tiled=True),
        lax.all_gather(up_a, "seq", axis=0, tiled=True),
        lax.all_gather(gate_b, "seq", axis=0, tiled=True),
        lax.all_gather(up_b, "seq", axis=0, tiled=True),
        lax.all_gather(down_a, "seq", axis=0, tiled=True),
        lax.all_gather(down_b, "seq", axis=0, tiled=True),
    )
    picker = (slot_used[:, None] == jnp.arange(adapters_n, dtype=jnp.int32)[None, :]).astype(
        jnp.bfloat16
    )
    fetched = tuple((choose(picker, stacked) for stacked in whole))
    fetch_ga, fetch_ua, fetch_gb, fetch_ub, fetch_da, fetch_db = fetched
    prompt_ends = jnp.cumsum(prompt_lengths[0])
    positions = jnp.arange(group_tok, dtype=jnp.int32)
    prompt_index = jnp.sum((positions[:, None] >= prompt_ends[None, :]).astype(jnp.int32), axis=1)
    prompts_n = prompt_lengths.shape[1]
    hits = prompt_index[:, None] == jnp.arange(prompts_n, dtype=jnp.int32)[None, :]
    tok_choice = jnp.sum(jnp.where(hits, prompt_choice[0][None, :], 0), axis=1)
    token_weights = (tok_choice[:, None] == jnp.arange(used_n, dtype=jnp.int32)[None, :]).astype(
        jnp.float32
    )
    row_first = lax.axis_index("tensor") * tok_dev
    own_weights = lax.dynamic_slice_in_dim(token_weights, row_first, tok_dev, 0)
    residual_float = resid[0].astype(jnp.float32)
    scale = lax.rsqrt(jnp.mean(residual_float * residual_float, axis=-1, keepdims=True) + 1e-06)
    normalized_input = (residual_float * scale * norm_gain.astype(jnp.float32)).astype(jnp.bfloat16)
    both_in = jnp.concatenate([to_columns(fetch_ga), to_columns(fetch_ua)], axis=1)
    col_first = lax.axis_index("tensor") * feat_loc
    piece = lax.all_gather(normalized_input, "tensor", axis=0, tiled=True)
    gate_part = jnp.dot(piece, gate_weight_matrix, preferred_element_type=jnp.float32)
    up_part = jnp.dot(piece, up_weight, preferred_element_type=jnp.float32)
    own_cols = lax.dynamic_slice_in_dim(piece, col_first, feat_loc, 1)
    low_part = jnp.dot(own_cols, both_in, preferred_element_type=jnp.float32)
    joined = jnp.concatenate([gate_part, up_part, low_part], axis=1)
    plain_output = joined[:, : 2 * hidden_local]
    low_rank = joined[:, 2 * hidden_local :].reshape(group_tok, 2, used_n, rank_n)
    partial_mid = jnp.sum(low_rank * token_weights[:, None, :, None], axis=2)
    mids = lax.psum(partial_mid.astype(jnp.bfloat16), "tensor")
    weights_bf = token_weights.astype(jnp.bfloat16)
    spread = (mids[:, :, None, :] * weights_bf[:, None, :, None]).reshape(
        group_tok, 2, used_n * rank_n
    )
    gate_adapter_rows = jnp.dot(
        spread[:, 0],
        fetch_gb.reshape(used_n * rank_n, hidden_local),
        preferred_element_type=jnp.float32,
    )
    up_adapter_rows = jnp.dot(
        spread[:, 1],
        fetch_ub.reshape(used_n * rank_n, hidden_local),
        preferred_element_type=jnp.float32,
    )
    gate_preactivation = plain_output[:, :hidden_local] + adapter_scale * gate_adapter_rows
    up_preactivation = plain_output[:, hidden_local:] + adapter_scale * up_adapter_rows
    hidden = (jax.nn.silu(gate_preactivation) * up_preactivation).astype(jnp.bfloat16)
    down_total_sum = lax.psum_scatter(
        jnp.dot(hidden, w_down, preferred_element_type=jnp.float32).astype(jnp.bfloat16),
        "tensor",
        scatter_dimension=0,
        tiled=True,
    ).astype(jnp.float32)
    down_adapter_rows = jnp.dot(
        hidden, to_columns(fetch_da), preferred_element_type=jnp.float32
    ).reshape(group_tok, used_n, rank_n)
    partial_down = jnp.sum(down_adapter_rows * token_weights[:, :, None], axis=1)
    mid_down = lax.psum_scatter(
        partial_down.astype(jnp.bfloat16), "tensor", scatter_dimension=0, tiled=True
    )
    spread_down = (mid_down[:, None, :] * own_weights.astype(jnp.bfloat16)[:, :, None]).reshape(
        tok_dev, used_n * rank_n
    )
    adapter_down_term = jnp.dot(
        spread_down,
        fetch_db.reshape(used_n * rank_n, fetch_db.shape[2]),
        preferred_element_type=jnp.float32,
    )
    return (residual_float + down_total_sum + adapter_scale * adapter_down_term).astype(
        jnp.bfloat16
    )[None]


def solution(mesh):
    placed = (
        P("seq", "tensor", None),
        P(),
        P(None, "tensor"),
        P(None, "tensor"),
        P("tensor", None),
        P("seq", "tensor", None),
        P("seq", None, "tensor"),
        P("seq", "tensor", None),
        P("seq", None, "tensor"),
        P("seq", "tensor", None),
        P("seq", None, None),
        P("seq", None),
        P("seq", None),
        P(),
        P(),
    )
    return jax.shard_map(
        local, mesh=mesh, in_specs=placed, out_specs=P("seq", "tensor", None), check_vma=False
    )
```

profile of v0, /device:TPU:1, one launch (start us, length us, event | category | flops | bytes accessed | tf_op | source)
XLA Modules:
  0.0 651.6 jit_solution(14810793064661548938)
XLA Ops:
  7.4 1.1 fusion.10
  9.2 1.5 fusion.12
  10.8 1.3 reduce-window.8
  12.1 39.2 %all_gather.22 = bf16[64,64,16]{1,2,0:T(8,128)(2,1)S(1)} all-gather(bf16[4,64,16]{1,2,0:T(8,128)(2,1)} %param.20), channel_id=1, replica_groups=mesh['tensor'=32,'seq'=16] {'seq'}, dimensions={0}, use_global_device_ids=true | all-gather | bytes 139264 | tf_op jit(solution)/shard_map/all_gather | solution.py:48
  51.8 0.9 select_reduce_fusion.1
  53.2 39.0 %all_gather.23 = bf16[64,64,16]{1,2,0:T(8,128)(2,1)S(1)} all-gather(bf16[4,64,16]{1,2,0:T(8,128)(2,1)} %param.22), channel_id=1, replica_groups=mesh['tensor'=32,'seq'=16] {'seq'}, dimensions={0}, use_global_device_ids=true | all-gather | bytes 139264 | tf_op jit(solution)/shard_map/all_gather | solution.py:49
  93.2 34.7 %all_gather.24 = bf16[64,16,342]{2,1,0:T(8,128)(2,1)S(1)} all-gather(bf16[4,16,342]{2,1,0:T(8,128)(2,1)S(1)} %copy-done.2), channel_id=1, replica_groups=mesh['tensor'=32,'seq'=16] {'seq'}, dimensions={0}, use_global_device_ids=true | all-gather | bytes 744192 | tf_op jit(solution)/shard_map/all_gather | solution.py:50
  129.2 35.9 %all_gather.25 = bf16[64,16,342]{2,1,0:T(8,128)(2,1)S(1)} all-gather(bf16[4,16,342]{2,1,0:T(8,128)(2,1)S(1)} %copy-done.3), channel_id=1, replica_groups=mesh['tensor'=32,'seq'=16] {'seq'}, dimensions={0}, use_global_device_ids=true | all-gather | bytes 744192 | tf_op jit(solution)/shard_map/all_gather | solution.py:51
  165.1 0.7 reshape.167
  166.1 1.0 reshape_reshape.10
  167.1 36.3 %all_gather.26 = bf16[64,342,16]{1,2,0:T(8,128)(2,1)} all-gather(bf16[4,342,16]{1,2,0:T(8,128)(2,1)S(1)} %copy-done.4), channel_id=1, replica_groups=mesh['tensor'=32,'seq'=16] {'seq'}, dimensions={0}, use_global_device_ids=true | all-gather | bytes 744192 | tf_op jit(solution)/shard_map/all_gather | solution.py:52
  203.4 2.4 copy.53
  206.3 1.1 reshape.169
  208.3 1.4 fusion.13
  209.8 195.1 %psum.7 = bf16[512,2,16]{0,2,1:T(8,128)(2,1)S(1)} all-reduce(bf16[512,2,16]{0,2,1:T(8,128)(2,1)S(1)} %multiply_reduce_fusion), channel_id=1, replica_groups=mesh['tensor'=32,'seq'=16] {'tensor'}, use_global_device_ids=true, to_apply=%region_6.7 | all-reduce | flops 16384 | bytes 65536 | tf_op jit(solution)/shard_map/psum | solution.py:85
  405.0 2.7 fusion.28
  408.1 0.9 fusion.29
  409.7 0.8 copy.57
  411.3 2.6 convolution_convert_fusion.4
  414.1 107.1 %reduce-scatter.7.cloned.1.call-done = bf16[16,16]{1,0:T(8,128)(2,1)} async-done(((bf16[512,16]{1,0:T(8,128)(2,1)}), bf16[16,16]{1,0:T(8,128)(2,1)}) %reduce-scatter.7.cloned.1.call-update) | async-done | bytes 528 | tf_op jit(solution)/shard_map/reduce_scatter | solution.py:113
  521.2 0.8 broadcast_multiply_fusion
  522.1 4.6 copy.59
  528.0 114.7 %reduce-scatter.5.cloned.1.call-done = bf16[16,2048]{1,0:T(8,128)(2,1)} async-done(((bf16[512,2048]{1,0:T(8,128)(2,1)}), bf16[16,2048]{1,0:T(8,128)(2,1)}) %reduce-scatter.5.cloned.1.call-update) | async-done | bytes 65552 | tf_op jit(solution)/shard_map/reduce_scatter | solution.py:103
  642.7 1.8 fusion.2
  (60 shorter events, 9.2 us)
Async XLA Ops:
  7.4 403.9 %copy-start = (bf16[342,2048]{1,0:T(8,128)(2,1)S(1)}, bf16[342,2048]{1,0:T(8,128)(2,1)}, u32[]{:S(2)}) copy-start(bf16[342,2048]{1,0:T(8,128)(2,1)} %param.19) | copy-start | bytes 4202500
  7.4 85.8 %copy-start.2 = (bf16[4,16,342]{2,1,0:T(8,128)(2,1)S(1)}, bf16[4,16,342]{2,1,0:T(8,128)(2,1)}, u32[]{:S(2)}) copy-start(bf16[4,16,342]{2,1,0:T(8,128)(2,1)} %param.21) | copy-start | bytes 131332
  7.4 200.9 %all-gather.3.cloned.1.call-start = ((), (), s32[]{:S(2)}) async-start(), calls=%async_computation.2 | async-start | bytes 2162688 | tf_op jit(solution)/shard_map/all_gather | solution.py:76
  10.7 510.4 %reduce-scatter.7.cloned.1.call-start = ((), (), s32[]{:S(2)}) async-start(), calls=%async_computation.5 | async-start | bytes 135168 | tf_op jit(solution)/shard_map/reduce_scatter | solution.py:113
  92.8 36.4 %copy-start.3 = (bf16[4,16,342]{2,1,0:T(8,128)(2,1)S(1)}, bf16[4,16,342]{2,1,0:T(8,128)(2,1)}, u32[]{:S(2)}) copy-start(bf16[4,16,342]{2,1,0:T(8,128)(2,1)} %param.23) | copy-start | bytes 131332
  128.9 38.2 %copy-start.4 = (bf16[4,342,16]{1,2,0:T(8,128)(2,1)S(1)}, bf16[4,342,16]{1,2,0:T(8,128)(2,1)}, u32[]{:S(2)}) copy-start(bf16[4,342,16]{1,2,0:T(8,128)(2,1)} %param.24) | copy-start | bytes 131332
  205.8 2.2 copy-start.7
  205.8 2.3 copy-start.6
  208.0 196.9 %copy-start.8 = (bf16[2048,342]{0,1:T(8,128)(2,1)S(1)}, bf16[2048,342]{0,1:T(8,128)(2,1)}, u32[]{:S(2)}) copy-start(bf16[2048,342]{0,1:T(8,128)(2,1)} %param.17) | copy-start | bytes 4202500
  405.0 3.0 copy-start.5
  405.0 3.0 copy-start.9
  408.1 0.9 copy-start.1
  410.5 111.6 %all-gather.5.cloned.1.call-start = ((), (), s32[]{:S(2)}) async-start(), calls=%async_computation.4 | async-start | bytes 4456448 | tf_op jit(solution)/shard_map/all_gather | solution.py:53
  411.1 231.6 %reduce-scatter.5.cloned.1.call-start = ((), (), s32[]{:S(2)}) async-start(), calls=%async_computation.3 | async-start | bytes 2162688 | tf_op jit(solution)/shard_map/reduce_scatter | solution.py:103
Sparse Core Ops, SparseCore 0:
  11.3 85.9 all-gather.2
  410.6 110.5 reduce-scatter.6
  525.6 117.0 reduce-scatter.4
Sparse Core Ops, SparseCore 1:
  413.0 89.7 all-gather.4
where the time goes:
time: 652 us
  blocking collectives  380 us (58%)
  waiting for transfers between devices  222 us (34%)
  between operations  14.9 us (2%)
  local copies, waits for them, and re-layouts  14.7 us (2%)
  matrix products  12.5 us (2%)
  other arithmetic  6.66 us (1%)
    psum x1, blocking collectives, local(): mids = lax.psum(partial_mid.astype(jnp.bfloat16), 'tensor')  195 us
    reduce_scatter x1, waiting for transfers between devices, local(): lax.psum_scatter(jnp.dot(hidden, w_down, preferred_element_type=jnp.float...  115 us
    reduce_scatter x1, waiting for transfers between devices, local(): lax.psum_scatter(partial_down.astype(jnp.bfloat16), 'tensor', scatter_dim...  107 us
    all_gather x1, blocking collectives, local(): lax.all_gather(gate_a, 'seq', axis=0, tiled=True)  39.2 us
    all_gather x1, blocking collectives, local(): lax.all_gather(up_a, 'seq', axis=0, tiled=True)  39 us
    all_gather x1, blocking collectives, local(): lax.all_gather(down_a, 'seq', axis=0, tiled=True)  36.3 us
    all_gather x1, blocking collectives, local(): lax.all_gather(up_b, 'seq', axis=0, tiled=True)  35.9 us
    all_gather x1, blocking collectives, local(): lax.all_gather(gate_b, 'seq', axis=0, tiled=True)  34.7 us
  transfers between devices with their start and end apart: 4, of which 2 were waited for; matrix products, arithmetic and copies ran while one was open for 3% of the time, Pallas kernels for 0%

commit v1 on v0

v1 whole, which is shorter than its diff:
```python
import jax
import jax.numpy as jnp
from jax import lax
from jax.sharding import PartitionSpec as P

adapter_scale = 0.5


def pick_rows(picker, stacked):
    flat = stacked.reshape(stacked.shape[0], -1)
    chosen = jnp.dot(picker, flat, preferred_element_type=jnp.float32).astype(jnp.bfloat16)
    return chosen.reshape((picker.shape[0],) + stacked.shape[1:])


def select_token(values, weights):
    return jnp.sum(values * weights[:, :, None], axis=1)


def local(
    resid,
    norm_gain,
    gate_weight_matrix,
    up_weight,
    w_down,
    gate_a,
    gate_b,
    up_a,
    up_b,
    down_a,
    down_b,
    prompt_lengths,
    prompt_choice,
    used_adapters,
    adapter_holder,
):
    tensor_n = lax.axis_size("tensor")
    tok_dev = resid.shape[1]
    d_model = resid.shape[2]
    group_tok = tok_dev * tensor_n
    used_n = used_adapters.shape[0]
    rank_n = gate_a.shape[2]
    feat_loc = gate_a.shape[1]
    slots_loc = gate_a.shape[0]
    hidden_local = gate_weight_matrix.shape[1]
    adapters_n = adapter_holder.shape[0]

    matches = used_adapters[:, None] == jnp.arange(adapters_n, dtype=jnp.int32)[None, :]
    slot_used = jnp.sum(jnp.where(matches, adapter_holder[None, :], 0), axis=1)
    picker = (slot_used[:, None] == jnp.arange(adapters_n, dtype=jnp.int32)[None, :]).astype(
        jnp.bfloat16
    )

    pieces = (gate_a, up_a, gate_b, up_b, down_a)
    widths = [p.shape[1] * p.shape[2] for p in pieces]
    pack = jnp.concatenate([p.reshape(slots_loc, -1) for p in pieces], axis=1)
    whole = lax.all_gather(pack, "seq", axis=0, tiled=True)
    chosen = pick_rows(picker, whole)
    offs = [0]
    for w in widths:
        offs.append(offs[-1] + w)
    sel = [
        chosen[:, offs[i] : offs[i + 1]].reshape((used_n,) + pieces[i].shape[1:])
        for i in range(len(pieces))
    ]
    sel_ga, sel_ua, sel_gb, sel_ub, sel_da = sel

    whole_db = lax.all_gather(down_b, "seq", axis=0, tiled=True)
    sel_db = pick_rows(picker, whole_db)

    prompt_ends = jnp.cumsum(prompt_lengths[0])
    positions = jnp.arange(group_tok, dtype=jnp.int32)
    prompt_index = jnp.sum((positions[:, None] >= prompt_ends[None, :]).astype(jnp.int32), axis=1)
    prompts_n = prompt_lengths.shape[1]
    hits = prompt_index[:, None] == jnp.arange(prompts_n, dtype=jnp.int32)[None, :]
    tok_choice = jnp.sum(jnp.where(hits, prompt_choice[0][None, :], 0), axis=1)
    token_weights = (tok_choice[:, None] == jnp.arange(used_n, dtype=jnp.int32)[None, :]).astype(
        jnp.float32
    )
    row_first = lax.axis_index("tensor") * tok_dev
    own_weights = lax.dynamic_slice_in_dim(token_weights, row_first, tok_dev, 0)

    residual_float = resid[0].astype(jnp.float32)
    scale = lax.rsqrt(jnp.mean(residual_float * residual_float, axis=-1, keepdims=True) + 1e-06)
    normalized_input = (residual_float * scale * norm_gain.astype(jnp.float32)).astype(jnp.bfloat16)

    tpack = jnp.concatenate(
        [normalized_input.reshape(-1), sel_ga.reshape(-1), sel_ua.reshape(-1)], axis=0
    )
    tall = lax.all_gather(tpack, "tensor", axis=0, tiled=False)
    n_tok_el = tok_dev * d_model
    n_a_el = used_n * feat_loc * rank_n
    piece = tall[:, :n_tok_el].reshape(group_tok, d_model)
    ga_all = tall[:, n_tok_el : n_tok_el + n_a_el].reshape(tensor_n, used_n, feat_loc, rank_n)
    ua_all = tall[:, n_tok_el + n_a_el :].reshape(tensor_n, used_n, feat_loc, rank_n)

    def to_cols(a):
        return jnp.transpose(a, (0, 2, 1, 3)).reshape(tensor_n * feat_loc, used_n * rank_n)

    both_in = jnp.concatenate([to_cols(ga_all), to_cols(ua_all)], axis=1)
    low = jnp.dot(piece, both_in, preferred_element_type=jnp.float32).reshape(
        group_tok, 2, used_n, rank_n
    )
    mid_gate = select_token(low[:, 0], token_weights).astype(jnp.bfloat16)
    mid_up = select_token(low[:, 1], token_weights).astype(jnp.bfloat16)
    weights_bf = token_weights.astype(jnp.bfloat16)

    def spread(mid):
        return (mid[:, None, :] * weights_bf[:, :, None]).reshape(group_tok, used_n * rank_n)

    gate_part = jnp.dot(piece, gate_weight_matrix, preferred_element_type=jnp.float32)
    up_part = jnp.dot(piece, up_weight, preferred_element_type=jnp.float32)
    gate_adapter_rows = jnp.dot(
        spread(mid_gate),
        sel_gb.reshape(used_n * rank_n, hidden_local),
        preferred_element_type=jnp.float32,
    )
    up_adapter_rows = jnp.dot(
        spread(mid_up),
        sel_ub.reshape(used_n * rank_n, hidden_local),
        preferred_element_type=jnp.float32,
    )
    gate_preactivation = gate_part + adapter_scale * gate_adapter_rows
    up_preactivation = up_part + adapter_scale * up_adapter_rows
    hidden = (jax.nn.silu(gate_preactivation) * up_preactivation).astype(jnp.bfloat16)

    down_part = jnp.dot(hidden, w_down, preferred_element_type=jnp.float32).astype(jnp.bfloat16)
    da_cols = jnp.transpose(sel_da, (1, 0, 2)).reshape(hidden_local, used_n * rank_n)
    down_adapter_rows = jnp.dot(hidden, da_cols, preferred_element_type=jnp.float32).reshape(
        group_tok, used_n, rank_n
    )
    partial_down = select_token(down_adapter_rows, token_weights).astype(jnp.bfloat16)

    joined = jnp.concatenate([down_part, partial_down], axis=1)
    reduced = lax.psum_scatter(joined, "tensor", scatter_dimension=0, tiled=True)
    down_total_sum = reduced[:, :d_model].astype(jnp.float32)
    mid_down = reduced[:, d_model:]

    spread_down = (mid_down[:, None, :] * own_weights.astype(jnp.bfloat16)[:, :, None]).reshape(
        tok_dev, used_n * rank_n
    )
    adapter_down_term = jnp.dot(
        spread_down,
        sel_db.reshape(used_n * rank_n, sel_db.shape[2]),
        preferred_element_type=jnp.float32,
    )
    return (residual_float + down_total_sum + adapter_scale * adapter_down_term).astype(
        jnp.bfloat16
    )[None]


def solution(mesh):
    placed = (
        P("seq", "tensor", None),
        P(),
        P(None, "tensor"),
        P(None, "tensor"),
        P("tensor", None),
        P("seq", "tensor", None),
        P("seq", None, "tensor"),
        P("seq", "tensor", None),
        P("seq", None, "tensor"),
        P("seq", "tensor", None),
        P("seq", None, None),
        P("seq", None),
        P("seq", None),
        P(),
        P(),
    )
    return jax.shard_map(
        local, mesh=mesh, in_specs=placed, out_specs=P("seq", "tensor", None), check_vma=False
    )
```

time: 652 us -> 428 us (0.66)
  blocking collectives: 380 us -> 0 us
  waiting for transfers between devices: 222 us -> 338 us
  local copies, waits for them, and re-layouts: 14.7 us -> 59.9 us
    all_gather x2 -> x3, waiting for transfers between devices: 0.04 us -> 212 us  [the longest x1 98.3 us: local(): tall = lax.all_gather(tpack, 'tensor', axis=0, tiled=False)]
    psum x1 -> x0, blocking collectives: 195 us -> none  [local(): mids = lax.psum(partial_mid.astype(jnp.bfloat16), 'tensor')]
    all_gather x5 -> x0, blocking collectives: 185 us -> none  [the longest x1 39.2 us: local(): lax.all_gather(gate_a, 'seq', axis=0, tiled=True)]
    reduce_scatter x2 -> x1, waiting for transfers between devices: 222 us -> 125 us  [local(): lax.psum_scatter(joined, 'tensor', scatter_dimension=0, tiled=True)]
    slice x0 -> x6, local copies, waits for them, and re-layouts: none -> 12.9 us  [the longest x2 5.75 us: local(): tall[:, n_tok_el:n_tok_el + n_a_el]]
    transpose x3, local copies, waits for them, and re-layouts: 0.9 us -> 11 us  [the longest x2 9.76 us: to_cols(): jnp.transpose(a, (0, 2, 1, 3)).reshape(tensor_n * feat_loc, used_n * rank_n)]
    reshape x5 -> x10, local copies, waits for them, and re-layouts: 3.03 us -> 13.1 us  [the longest x2 4.88 us: to_cols(): jnp.transpose(a, (0, 2, 1, 3)).reshape(tensor_n * feat_loc, used_n * rank_n)]
    unnamed x22 -> x43, local copies, waits for them, and re-layouts: 5.39 us -> 13.5 us
  transfers between devices with their start and end apart: 4 -> 4, of which waited for: 2 -> 4; matrix products, arithmetic and copies ran while one was open for 3% -> 14% of each run, Pallas kernels for 0% -> 0%
where the time goes in v1:
time: 428 us; the launch traced here: 427 us
  waiting for transfers between devices  338 us (79%)
  local copies, waits for them, and re-layouts  59.9 us (14%)
  between operations  13.5 us (3%)
  matrix products  10 us (2%)
  other arithmetic  5.85 us (1%)
    reduce_scatter x1, waiting for transfers between devices, local(): lax.psum_scatter(joined, 'tensor', scatter_dimension=0, tiled=True)  125 us
    all_gather x1, waiting for transfers between devices, local(): tall = lax.all_gather(tpack, 'tensor', axis=0, tiled=False)  98.3 us
    all_gather x1, waiting for transfers between devices, local(): whole = lax.all_gather(pack, 'seq', axis=0, tiled=True)  82.9 us
    all_gather x1, waiting for transfers between devices, local(): whole_db = lax.all_gather(down_b, 'seq', axis=0, tiled=True)  30.6 us
    unnamed x43, local copies, waits for them, and re-layouts  13.5 us
    transpose x2, local copies, waits for them, and re-layouts, to_cols(): jnp.transpose(a, (0, 2, 1, 3)).reshape(tensor_n * feat_loc, used_n * rank_n)  9.76 us
  transfers between devices with their start and end apart: 4, of which 4 were waited for; matrix products, arithmetic and copies ran while one was open for 14% of the time, Pallas kernels for 0%

profile of v1, /device:TPU:1, one launch (start us, length us, event | category | flops | bytes accessed | tf_op | source)
XLA Modules:
  0.0 427.0 jit_solution(15833528576533599783)
XLA Ops:
  14.0 82.9 %all-gather.10.cloned.1.call-done = bf16[16,4,18464]{2,1,0:T(4,128)(2,1)} async-done(((bf16[1,4,18464]{2,1,0:T(4,128)(2,1)}), bf16[16,4,18464]{2,1,0:T(4,128)(2,1)}) %all-gather.10.cloned.1.call-update) | async-done | bytes 2363408 | tf_op jit(solution)/shard_map/all_gather | solution.py:56
  96.9 4.3 %reshape.194 = bf16[64,18464]{1,0:T(8,128)(2,1)} reshape(bf16[16,4,18464]{2,1,0:T(4,128)(2,1)} %all-gather.10.cloned.1.call-done) | data formatting | bytes 4726784
  101.3 2.2 convolution_convert_fusion.1
  108.5 1.2 copy.52
  109.8 98.3 %all-gather.8.cloned.1.call-done = bf16[2097152]{0:T(1024)(128)(2,1)} async-done(((bf16[65536]{0:T(1024)(128)(2,1)}), bf16[2097152]{0:T(1024)(128)(2,1)}) %all-gather.8.cloned.1.call-update) | async-done | bytes 4194320 | tf_op jit(solution)/shard_map/all_gather | solution.py:89
  208.1 5.5 %reshape.192 = bf16[32,65536]{1,0:T(8,128)(2,1)} reshape(bf16[2097152]{0:T(1024)(128)(2,1)} %all-gather.8.cloned.1.call-done) | data formatting | bytes 8388608 | tf_op jit(solution)/shard_map/all_gather | solution.py:89
  213.6 1.7 slice.50
  215.3 2.4 reshape.195
  217.7 2.4 reshape.180
  220.1 2.7 fusion.23
  222.8 3.1 copy.48
  225.9 4.9 %copy.49 = bf16[32,64,16,16]{1,0,3,2:T(8,128)(2,1)S(1)} copy(bf16[32,64,16,16]{0,3,1,2:T(8,128)(2,1)} %bitcast.93) | data formatting | bytes 2097152 | tf_op jit(solution)/shard_map/transpose | solution.py:97
  230.7 2.4 reshape.182
  233.2 4.6 %copy.50 = bf16[32,16384]{0,1:T(8,128)(2,1)} copy(bf16[32,16384]{1,0:T(8,128)(2,1)} %get-tuple-element.8) | data formatting | bytes 2097152 | tf_op jit(solution)/shard_map/slice | solution.py:94
  237.8 4.9 %copy.51 = bf16[32,64,16,16]{1,0,3,2:T(8,128)(2,1)S(1)} copy(bf16[32,64,16,16]{0,3,1,2:T(8,128)(2,1)} %bitcast.94) | data formatting | bytes 2097152 | tf_op jit(solution)/shard_map/transpose | solution.py:97
  242.7 2.4 reshape.184
  245.1 1.9 pad_maximum_fusion.1
  247.4 1.3 fusion.3
  253.1 1.3 convolution_convert_fusion.2
  254.4 1.6 pad_maximum_fusion
  256.2 30.6 %all-gather.6.cloned.1.call-done = bf16[64,16,2048]{2,1,0:T(8,128)(2,1)} async-done(((bf16[4,16,2048]{2,1,0:T(8,128)(2,1)}), bf16[64,16,2048]{2,1,0:T(8,128)(2,1)}) %all-gather.6.cloned.1.call-update) | async-done | bytes 4194320 | tf_op jit(solution)/shard_map/all_gather | solution.py:67
  286.8 4.6 %copy.61 = bf16[8,8,16,2048]{3,1,2,0:T(8,128)(2,1)S(1)} copy(bf16[8,8,16,2048]{3,2,1,0:T(8,128)(2,1)} %bitcast.97) | data formatting | bytes 8388608
  292.7 125.2 %reduce-scatter.2.cloned.1.call-done = bf16[16,2064]{1,0:T(8,128)(2,1)} async-done(((bf16[512,2064]{1,0:T(8,128)(2,1)}), bf16[16,2064]{1,0:T(8,128)(2,1)}) %reduce-scatter.2.cloned.1.call-update) | async-done | bytes 66064 | tf_op jit(solution)/shard_map/reduce_scatter | solution.py:134
  418.7 1.8 fusion.2
  (85 shorter events, 19.4 us)
Async XLA Ops:
  6.5 246.6 %copy-start = (bf16[342,2048]{1,0:T(8,128)(2,1)S(1)}, bf16[342,2048]{1,0:T(8,128)(2,1)}, u32[]{:S(2)}) copy-start(bf16[342,2048]{1,0:T(8,128)(2,1)} %param.19) | copy-start | bytes 4202500
  6.5 6.9 %copy-start.4 = (bf16[1,16,2048]{2,1,0:T(8,128)(2,1)S(1)}, bf16[1,16,2048]{2,1,0:T(8,128)(2,1)}, u32[]{:S(2)}) copy-start(bf16[1,16,2048]{2,1,0:T(8,128)(2,1)} %param.15) | copy-start | bytes 196612
  6.5 7.3 %copy-start.13 = (s32[16]{0:T(128)S(1)}, s32[16]{0:T(128)}, u32[]{:S(2)}) copy-start(s32[16]{0:T(128)} %param.28) | copy-start | bytes 196
  6.5 7.3 %copy-start.12 = (s32[64]{0:T(128)S(1)}, s32[64]{0:T(128)}, u32[]{:S(2)}) copy-start(s32[64]{0:T(128)} %param.29) | copy-start | bytes 772
  6.5 90.4 %all-gather.10.cloned.1.call-start = ((), (), s32[]{:S(2)}) async-start(), calls=%async_computation.4 | async-start | bytes 2524160 | tf_op jit(solution)/shard_map/all_gather | solution.py:56
  12.7 195.4 %all-gather.8.cloned.1.call-start = ((), (), s32[]{:S(2)}) async-start(), calls=%async_computation.3 | async-start | bytes 4325376 | tf_op jit(solution)/shard_map/all_gather | solution.py:89
  14.0 87.3 %copy-start.7 = (s32[16]{0:T(128)}, s32[16]{0:T(128)S(1)}, u32[]{:S(2)}) copy-start(s32[16]{0:T(128)S(1)} %select_reduce_fusion.1) | copy-start | bytes 196
  101.3 3.7 copy-start.14
  101.3 4.0 copy-start.9
  104.2 182.6 %all-gather.6.cloned.1.call-start = ((), (), s32[]{:S(2)}) async-start(), calls=%async_computation.2 | async-start | bytes 4456448 | tf_op jit(solution)/shard_map/all_gather | solution.py:67
  104.9 312.9 %reduce-scatter.2.cloned.1.call-start = ((), (), s32[]{:S(2)}) async-start(), calls=%async_computation.1 | async-start | bytes 2297856 | tf_op jit(solution)/shard_map/reduce_scatter | solution.py:134
  245.1 2.3 copy-start.2
  247.4 1.6 copy-start.1
  247.4 2.0 copy-start.10
  249.4 0.9 copy-start.3
  249.4 1.5 copy-start.11
  250.8 0.9 copy-start.6
  251.8 0.9 copy-start.5
  286.8 4.6 %copy-start.8 = (s32[16]{0:T(128)S(1)}, s32[16]{0:T(128)}, u32[]{:S(2)}) copy-start(s32[16]{0:T(128)} %copy-done.7) | copy-start | bytes 196
Sparse Core Ops, SparseCore 0:
  12.8 84.0 all-gather.9
  104.3 103.7 all-gather.7
  210.2 76.5 all-gather.5
  291.3 126.5 reduce-scatter.1

commit v2 on v1

--- a/solution.py
+++ b/solution.py
@@ -50,11 +50,18 @@
         jnp.bfloat16
     )
 
-    pieces = (gate_a, up_a, gate_b, up_b, down_a)
+    col_n = d_model // tensor_n
+    col_first = lax.axis_index("tensor") * col_n
+    db_block = lax.dynamic_slice_in_dim(down_b, col_first, col_n, 2)
+    pieces = (gate_a, up_a, gate_b, up_b, down_a, db_block)
     widths = [p.shape[1] * p.shape[2] for p in pieces]
     pack = jnp.concatenate([p.reshape(slots_loc, -1) for p in pieces], axis=1)
-    whole = lax.all_gather(pack, "seq", axis=0, tiled=True)
-    chosen = pick_rows(picker, whole)
+    whole = lax.all_gather(pack, "seq", axis=0, tiled=False)
+    seq_n = whole.shape[0]
+    picker3 = picker.reshape(used_n, seq_n, slots_loc)
+    chosen = jnp.einsum(
+        "ugs,gsx->ux", picker3, whole, preferred_element_type=jnp.float32
+    ).astype(jnp.bfloat16)
     offs = [0]
     for w in widths:
         offs.append(offs[-1] + w)
@@ -62,10 +69,7 @@
         chosen[:, offs[i] : offs[i + 1]].reshape((used_n,) + pieces[i].shape[1:])
         for i in range(len(pieces))
     ]
-    sel_ga, sel_ua, sel_gb, sel_ub, sel_da = sel
-
-    whole_db = lax.all_gather(down_b, "seq", axis=0, tiled=True)
-    sel_db = pick_rows(picker, whole_db)
+    sel_ga, sel_ua, sel_gb, sel_ub, sel_da, sel_db = sel
 
     prompt_ends = jnp.cumsum(prompt_lengths[0])
     positions = jnp.arange(group_tok, dtype=jnp.int32)
@@ -83,20 +87,19 @@
     scale = lax.rsqrt(jnp.mean(residual_float * residual_float, axis=-1, keepdims=True) + 1e-06)
     normalized_input = (residual_float * scale * norm_gain.astype(jnp.float32)).astype(jnp.bfloat16)
 
-    tpack = jnp.concatenate(
-        [normalized_input.reshape(-1), sel_ga.reshape(-1), sel_ua.reshape(-1)], axis=0
-    )
+    def feat_major(a):
+        return jnp.transpose(a, (1, 0, 2)).reshape(feat_loc, used_n * rank_n)
+
+    a_rows = jnp.concatenate([feat_major(sel_ga), feat_major(sel_ua)], axis=1).reshape(-1, d_model)
+    db_rows = sel_db.reshape(-1, d_model)
+    tpack = jnp.concatenate([normalized_input, a_rows, db_rows], axis=0)
     tall = lax.all_gather(tpack, "tensor", axis=0, tiled=False)
-    n_tok_el = tok_dev * d_model
-    n_a_el = used_n * feat_loc * rank_n
-    piece = tall[:, :n_tok_el].reshape(group_tok, d_model)
-    ga_all = tall[:, n_tok_el : n_tok_el + n_a_el].reshape(tensor_n, used_n, feat_loc, rank_n)
-    ua_all = tall[:, n_tok_el + n_a_el :].reshape(tensor_n, used_n, feat_loc, rank_n)
+    r0 = tok_dev
+    r1 = r0 + a_rows.shape[0]
+    piece = tall[:, :r0].reshape(group_tok, d_model)
+    both_in = tall[:, r0:r1].reshape(tensor_n * feat_loc, 2 * used_n * rank_n)
+    db_all = tall[:, r1:].reshape(tensor_n, used_n * rank_n, col_n)
 
-    def to_cols(a):
-        return jnp.transpose(a, (0, 2, 1, 3)).reshape(tensor_n * feat_loc, used_n * rank_n)
-
-    both_in = jnp.concatenate([to_cols(ga_all), to_cols(ua_all)], axis=1)
     low = jnp.dot(piece, both_in, preferred_element_type=jnp.float32).reshape(
         group_tok, 2, used_n, rank_n
     )
@@ -138,11 +141,9 @@
     spread_down = (mid_down[:, None, :] * own_weights.astype(jnp.bfloat16)[:, :, None]).reshape(
         tok_dev, used_n * rank_n
     )
-    adapter_down_term = jnp.dot(
-        spread_down,
-        sel_db.reshape(used_n * rank_n, sel_db.shape[2]),
-        preferred_element_type=jnp.float32,
-    )
+    adapter_down_term = jnp.einsum(
+        "tk,jkc->tjc", spread_down, db_all, preferred_element_type=jnp.float32
+    ).reshape(tok_dev, d_model)
     return (residual_float + down_total_sum + adapter_scale * adapter_down_term).astype(
         jnp.bfloat16
     )[None]

time: 428 us -> 364 us (0.85)
  waiting for transfers between devices: 338 us -> 298 us
  local copies, waits for them, and re-layouts: 59.9 us -> 32.3 us
    all_gather x2 -> x1, waiting for transfers between devices: 113 us -> 80.5 us  [local(): whole = lax.all_gather(pack, 'seq', axis=0, tiled=False)]
    reduce_scatter x1, waiting for transfers between devices: 125 us -> 107 us  [local(): lax.psum_scatter(joined, 'tensor', scatter_dimension=0, tiled=True)]
    all_gather x1, waiting for transfers between devices: 98.3 us -> 111 us  [local(): tall = lax.all_gather(tpack, 'tensor', axis=0, tiled=False)]
    unnamed x43 -> x21, local copies, waits for them, and re-layouts: 13.5 us -> 3.83 us
    transpose x2, local copies, waits for them, and re-layouts: 9.76 us -> 0.26 us  [feat_major(): return jnp.transpose(a, (1, 0, 2)).reshape(feat_loc, used_n * rank_n)]
    all_gather x1 -> x0, local copies, waits for them, and re-layouts: 5.52 us -> none  [local(): tall = lax.all_gather(tpack, 'tensor', axis=0, tiled=False)]
    slice x4 -> x2, local copies, waits for them, and re-layouts: 12 us -> 7.17 us  [the longest x1 4.83 us: local(): both_in = tall[:, r0:r1].reshape(tensor_n * feat_loc, 2 * used_n * rank_n)]
    reshape x4 -> x3, local copies, waits for them, and re-layouts: 9.68 us -> 6.48 us  [the longest x1 3.33 us: local(): db_all = tall[:, r1:].reshape(tensor_n, used_n * rank_n, col_n)]
  transfers between devices with their start and end apart: 4 -> 3, of which waited for: 4 -> 3; matrix products, arithmetic and copies ran while one was open for 14% -> 4% of each run, Pallas kernels for 0% -> 0%
where the time goes in v2:
time: 364 us; the launch traced here: 363 us
  waiting for transfers between devices  298 us (82%)
  local copies, waits for them, and re-layouts  32.3 us (9%)
  between operations  13.4 us (4%)
  matrix products  12.5 us (3%)
  other arithmetic  6.36 us (2%)
    all_gather x1, waiting for transfers between devices, local(): tall = lax.all_gather(tpack, 'tensor', axis=0, tiled=False)  111 us
    reduce_scatter x1, waiting for transfers between devices, local(): lax.psum_scatter(joined, 'tensor', scatter_dimension=0, tiled=True)  107 us
    all_gather x1, waiting for transfers between devices, local(): whole = lax.all_gather(pack, 'seq', axis=0, tiled=False)  80.5 us
  transfers between devices with their start and end apart: 3, of which 3 were waited for; matrix products, arithmetic and copies ran while one was open for 4% of the time, Pallas kernels for 0%

profile of v2, /device:TPU:1, one launch (start us, length us, event | category | flops | bytes accessed | tf_op | source)
XLA Modules:
  0.0 363.3 jit_solution(14223055320031481625)
XLA Ops:
  8.5 0.9 reshape.198
  11.3 1.0 copy.46
  12.6 0.9 concatenate.12
  15.1 1.0 fusion.16
  17.1 80.5 %all-gather.8.cloned.1.call-done = bf16[16,4,19488]{2,1,0:T(4,128)(2,1)} async-done(((bf16[1,4,19488]{2,1,0:T(4,128)(2,1)}), bf16[16,4,19488]{2,1,0:T(4,128)(2,1)}) %all-gather.8.cloned.1.call-update) | async-done | bytes 2494480 | tf_op jit(solution)/shard_map/all_gather | solution.py:59
  97.6 2.7 fusion
  102.8 1.0 reshape_reshape.11
  103.8 1.0 reshape_reshape.10
  104.8 1.0 reshape.210
  105.8 1.2 copy.52
  107.0 111.1 %all-gather.6.cloned.1.call-done = bf16[1280,2048]{1,0:T(8,128)(2,1)} async-done(((bf16[40,2048]{1,0:T(8,128)(2,1)}), bf16[1280,2048]{1,0:T(8,128)(2,1)}) %all-gather.6.cloned.1.call-update) | async-done | bytes 5242896 | tf_op jit(solution)/shard_map/all_gather | solution.py:96
  218.2 4.8 %fusion.24 = (bf16[32,16,2048]{2,1,0:T(8,128)(2,1)}, bf16[32,16,2048]{2,1,0:T(8,128)(2,1)}) fusion(bf16[32,40,2048]{2,1,0:T(8,128)(2,1)} %bitcast.71), kind=kLoop, calls=%fused_computation.52 | loop fusion | bytes 8388608 | tf_op jit(solution)/shard_map/slice | solution.py:100
  223.0 3.1 reshape.207
  226.1 2.5 copy.51
  228.6 3.1 fusion.29
  231.7 1.0 fusion.27
  233.3 1.3 fusion.28
  236.4 1.3 convolution_convert_fusion
  237.7 1.6 pad_maximum_fusion
  239.5 2.3 slice.64
  241.8 3.3 reshape.212
  245.2 1.6 copy.55
  246.8 106.8 %reduce-scatter.2.cloned.1.call-done = bf16[16,2064]{1,0:T(8,128)(2,1)} async-done(((bf16[512,2064]{1,0:T(8,128)(2,1)}), bf16[16,2064]{1,0:T(8,128)(2,1)}) %reduce-scatter.2.cloned.1.call-update) | async-done | bytes 66064 | tf_op jit(solution)/shard_map/reduce_scatter | solution.py:137
  354.5 2.3 fusion.4
  (63 shorter events, 12.6 us)
Async XLA Ops:
  6.5 229.9 %copy-start = (bf16[342,2048]{1,0:T(8,128)(2,1)S(1)}, bf16[342,2048]{1,0:T(8,128)(2,1)}, u32[]{:S(2)}) copy-start(bf16[342,2048]{1,0:T(8,128)(2,1)} %param.19) | copy-start | bytes 4202500
  6.5 91.0 %all-gather.8.cloned.1.call-start = ((), (), s32[]{:S(2)}) async-start(), calls=%async_computation.3 | async-start | bytes 2663424 | tf_op jit(solution)/shard_map/all_gather | solution.py:59
  13.5 204.6 %all-gather.6.cloned.1.call-start = ((), (), s32[]{:S(2)}) async-start(), calls=%async_computation.2 | async-start | bytes 5406720 | tf_op jit(solution)/shard_map/all_gather | solution.py:96
  100.3 2.0 copy-start.8
  100.3 2.3 copy-start.6
  102.0 251.6 %reduce-scatter.2.cloned.1.call-start = ((), (), s32[]{:S(2)}) async-start(), calls=%async_computation.1 | async-start | bytes 2297856 | tf_op jit(solution)/shard_map/reduce_scatter | solution.py:137
  228.6 3.1 copy-start.2
  228.6 3.1 copy-start.7
  231.7 1.6 copy-start.1
  233.3 1.5 copy-start.3
  234.5 0.9 copy-start.5
  235.0 1.0 copy-start.4
Sparse Core Ops, SparseCore 0:
  13.7 83.8 all-gather.7
  102.1 115.9 all-gather.5
  239.5 114.0 reduce-scatter.1

commit v3 on v2

--- a/solution.py
+++ b/solution.py
@@ -14,6 +14,22 @@
 
 def select_token(values, weights):
     return jnp.sum(values * weights[:, :, None], axis=1)
+
+
+def reduce_scatter_rows(x, axis_name, axis_n):
+    bits = axis_n.bit_length() - 1
+    me = lax.axis_index(axis_name)
+    rows = x.shape[0] // axis_n
+    acc = x.astype(jnp.float32).reshape((2,) * bits + (rows,) + x.shape[1:])
+    for b in range(bits):
+        ax = bits - 1 - b
+        mine = (me >> b) & 1
+        keep = lax.dynamic_index_in_dim(acc, mine, axis=ax, keepdims=False)
+        send = lax.dynamic_index_in_dim(acc, 1 - mine, axis=ax, keepdims=False)
+        perm = [(i, i ^ (1 << b)) for i in range(axis_n)]
+        got = lax.ppermute(send.astype(jnp.bfloat16), axis_name, perm)
+        acc = keep + got.astype(jnp.float32)
+    return acc
 
 
 def local(
@@ -134,9 +150,9 @@
     partial_down = select_token(down_adapter_rows, token_weights).astype(jnp.bfloat16)
 
     joined = jnp.concatenate([down_part, partial_down], axis=1)
-    reduced = lax.psum_scatter(joined, "tensor", scatter_dimension=0, tiled=True)
-    down_total_sum = reduced[:, :d_model].astype(jnp.float32)
-    mid_down = reduced[:, d_model:]
+    reduced = reduce_scatter_rows(joined, "tensor", tensor_n)
+    down_total_sum = reduced[:, :d_model]
+    mid_down = reduced[:, d_model:].astype(jnp.bfloat16)
 
     spread_down = (mid_down[:, None, :] * own_weights.astype(jnp.bfloat16)[:, :, None]).reshape(
         tok_dev, used_n * rank_n

time: 364 us -> 320 us (0.88)
  waiting for transfers between devices: 298 us -> 230 us
  starting transfers between devices: 0.27 us -> 16.4 us
  local copies, waits for them, and re-layouts: 32.3 us -> 36.9 us
    reduce_scatter x1 -> x0, waiting for transfers between devices: 107 us -> none  [local(): lax.psum_scatter(joined, 'tensor', scatter_dimension=0, tiled=True)]
    ppermute x0 -> x5, waiting for transfers between devices: none -> 37.8 us  [reduce_scatter_rows(): got = lax.ppermute(send.astype(jnp.bfloat16), axis_name, perm)]
    ppermute x0 -> x5, starting transfers between devices: none -> 16.4 us  [reduce_scatter_rows(): got = lax.ppermute(send.astype(jnp.bfloat16), axis_name, perm)]
    add x0 -> x5, other arithmetic: none -> 4.55 us  [reduce_scatter_rows(): acc = keep + got.astype(jnp.float32)]
    unnamed x21 -> x27, local copies, waits for them, and re-layouts: 3.83 us -> 8.03 us
  transfers between devices with their start and end apart: 3 -> 7, of which waited for: 3 -> 7; matrix products, arithmetic and copies ran while one was open for 4% -> 5% of each run, Pallas kernels for 0% -> 0%
where the time goes in v3:
time: 320 us; the launch traced here: 319 us
  waiting for transfers between devices  230 us (72%)
  local copies, waits for them, and re-layouts  36.9 us (12%)
  starting transfers between devices  16.4 us (5%)
  between operations  13.8 us (4%)
  matrix products  12.5 us (4%)
  other arithmetic  9.81 us (3%)
    all_gather x1, waiting for transfers between devices, local(): tall = lax.all_gather(tpack, 'tensor', axis=0, tiled=False)  111 us
    all_gather x1, waiting for transfers between devices, local(): whole = lax.all_gather(pack, 'seq', axis=0, tiled=False)  80.5 us
    ppermute x5, waiting for transfers between devices, reduce_scatter_rows(): got = lax.ppermute(send.astype(jnp.bfloat16), axis_name, perm)  37.8 us
    ppermute x5, starting transfers between devices, reduce_scatter_rows(): got = lax.ppermute(send.astype(jnp.bfloat16), axis_name, perm)  16.4 us
    unnamed x27, local copies, waits for them, and re-layouts  8.03 us
  transfers between devices with their start and end apart: 7, of which 7 were waited for; matrix products, arithmetic and copies ran while one was open for 5% of the time, Pallas kernels for 0%

profile of v3, /device:TPU:1, one launch (start us, length us, event | category | flops | bytes accessed | tf_op | source)
XLA Modules:
  0.0 319.2 jit_solution(15038001497240362538)
XLA Ops:
  17.0 80.5 %all-gather.8.cloned.1.call-done = bf16[16,4,19488]{2,1,0:T(4,128)(2,1)} async-done(((bf16[1,4,19488]{2,1,0:T(4,128)(2,1)}), bf16[16,4,19488]{2,1,0:T(4,128)(2,1)}) %all-gather.8.cloned.1.call-update) | async-done | bytes 2494480 | tf_op jit(solution)/shard_map/all_gather | solution.py:75
  97.6 2.7 fusion
  106.8 111.4 %all-gather.6.cloned.1.call-done = bf16[1280,2048]{1,0:T(8,128)(2,1)} async-done(((bf16[40,2048]{1,0:T(8,128)(2,1)}), bf16[1280,2048]{1,0:T(8,128)(2,1)}) %all-gather.6.cloned.1.call-update) | async-done | bytes 5242896 | tf_op jit(solution)/shard_map/all_gather | solution.py:112
  218.2 4.8 %fusion.29 = (bf16[32,16,2048]{2,1,0:T(8,128)(2,1)}, bf16[32,16,2048]{2,1,0:T(8,128)(2,1)}) fusion(bf16[32,40,2048]{2,1,0:T(8,128)(2,1)} %bitcast.94), kind=kLoop, calls=%fused_computation.68 | loop fusion | bytes 8388608 | tf_op jit(solution)/shard_map/slice | solution.py:116
  223.0 3.1 reshape.217
  226.1 2.5 copy.55
  228.6 3.1 fusion.34
  238.4 2.1 copy-done.1
  240.7 2.2 collective-permute-start
  242.8 2.6 collective-permute-done
  245.4 2.2 bitcast_add_fusion
  247.6 1.4 copy-done.2
  249.1 3.3 %collective-permute-start.1 = (bf16[2,2,2,16,2064]{4,3,0,1,2:T(8,128)(2,1)S(1)}, bf16[2,2,2,16,2064]{4,3,0,1,2:T(8,128)(2,1)S(1)}, u32[]{:S(2)}, u32[]{:S(2)}) collective-permute-start(bf16[2,2,2,16,2064]{4,3,0,1,2:T(8,128)(2,1)S(1)} %fusion.8), channel_id=1, source_target_pairs={{0,32},{16,48},{32,0},{48,16},{64,96},{80,112},{96,64},{112,80},{1... | collective-permute-start | bytes 1585160 | tf_op jit(solution)/shard_map/ppermute | solution.py:30
  252.4 12.5 %collective-permute-done.1 = bf16[2,2,2,16,2064]{4,3,0,1,2:T(8,128)(2,1)S(1)} collective-permute-done((bf16[2,2,2,16,2064]{4,3,0,1,2:T(8,128)(2,1)S(1)}, bf16[2,2,2,16,2064]{4,3,0,1,2:T(8,128)(2,1)S(1)}, u32[]{:S(2)}, u32[]{:S(2)}) %collective-permute-start.1) | collective-permute-done | bytes 528416 | tf_op jit(solution)/shard_map/ppermute | solution.py:30
  266.3 4.6 %collective-permute-start.2 = (bf16[2,2,16,2064]{3,2,0,1:T(8,128)(2,1)S(1)}, bf16[2,2,16,2064]{3,2,0,1:T(8,128)(2,1)S(1)}, u32[]{:S(2)}, u32[]{:S(2)}) collective-permute-start(bf16[2,2,16,2064]{3,2,0,1:T(8,128)(2,1)S(1)} %fusion.14), channel_id=1, source_target_pairs={{0,64},{16,80},{32,96},{48,112},{64,0},{80,16},{96,32},{112,48},{1... | collective-permute-start | bytes 792584 | tf_op jit(solution)/shard_map/ppermute | solution.py:30
  271.0 5.9 %collective-permute-done.2 = bf16[2,2,16,2064]{3,2,0,1:T(8,128)(2,1)S(1)} collective-permute-done((bf16[2,2,16,2064]{3,2,0,1:T(8,128)(2,1)S(1)}, bf16[2,2,16,2064]{3,2,0,1:T(8,128)(2,1)S(1)}, u32[]{:S(2)}, u32[]{:S(2)}) %collective-permute-start.2) | collective-permute-done | bytes 264224 | tf_op jit(solution)/shard_map/ppermute | solution.py:30
  276.9 3.5 %collective-permute-start.3 = (bf16[2,16,2064]{2,1,0:T(8,128)(2,1)S(1)}, bf16[2,16,2064]{2,1,0:T(8,128)(2,1)S(1)}, u32[]{:S(2)}, u32[]{:S(2)}) collective-permute-start(bf16[2,16,2064]{2,1,0:T(8,128)(2,1)S(1)} %fusion.16), channel_id=1, source_target_pairs={{0,128},{16,144},{32,160},{48,176},{64,192},{80,208},{96,224},{112... | collective-permute-start | bytes 396296 | tf_op jit(solution)/shard_map/ppermute | solution.py:30
  280.5 12.7 %collective-permute-done.3 = bf16[2,16,2064]{2,1,0:T(8,128)(2,1)S(1)} collective-permute-done((bf16[2,16,2064]{2,1,0:T(8,128)(2,1)S(1)}, bf16[2,16,2064]{2,1,0:T(8,128)(2,1)S(1)}, u32[]{:S(2)}, u32[]{:S(2)}) %collective-permute-start.3) | collective-permute-done | bytes 132128 | tf_op jit(solution)/shard_map/ppermute | solution.py:30
  294.5 2.7 collective-permute-start.4
  297.4 2.3 slice.65
  299.7 3.3 %reshape.222 = bf16[32,256,64]{2,1,0:T(8,128)(2,1)S(1)} reshape(bf16[32,8,2048]{2,1,0:T(8,128)(2,1)} %slice.65) | data formatting | bytes 2097152 | tf_op jit(solution)/shard_map/reshape | solution.py:117
  303.1 1.6 copy.60
  304.7 4.2 %collective-permute-done.4 = bf16[16,2064]{1,0:T(8,128)(2,1)} collective-permute-done((bf16[16,2064]{1,0:T(8,128)(2,1)}, bf16[16,2064]{1,0:T(8,128)(2,1)}, u32[]{:S(2)}, u32[]{:S(2)}) %collective-permute-start.4) | collective-permute-done | bytes 66080 | tf_op jit(solution)/shard_map/ppermute | solution.py:30
  310.1 2.2 fusion.23
  (87 shorter events, 27.9 us)
Async XLA Ops:
  6.5 230.1 %copy-start = (bf16[342,2048]{1,0:T(8,128)(2,1)S(1)}, bf16[342,2048]{1,0:T(8,128)(2,1)}, u32[]{:S(2)}) copy-start(bf16[342,2048]{1,0:T(8,128)(2,1)} %param.19) | copy-start | bytes 4202500
  6.5 91.0 %all-gather.8.cloned.1.call-start = ((), (), s32[]{:S(2)}) async-start(), calls=%async_computation.1 | async-start | bytes 2663424 | tf_op jit(solution)/shard_map/all_gather | solution.py:75
  13.5 204.6 %all-gather.6.cloned.1.call-start = ((), (), s32[]{:S(2)}) async-start(), calls=%async_computation | async-start | bytes 5406720 | tf_op jit(solution)/shard_map/all_gather | solution.py:112
  100.3 1.8 copy-start.11
  100.3 2.0 copy-start.9
  228.6 3.1 copy-start.4
  228.6 3.1 copy-start.10
  231.7 1.6 copy-start.3
  233.2 1.5 copy-start.6
  234.5 0.9 copy-start.8
  235.0 1.0 copy-start.7
  238.4 2.1 copy-start.1
  240.7 4.8 %collective-permute-start = (bf16[2,2,2,2,16,2064]{5,4,0,1,2,3:T(8,128)(2,1)S(1)}, bf16[2,2,2,2,16,2064]{5,4,0,1,2,3:T(8,128)(2,1)}, u32[]{:S(2)}, u32[]{:S(2)}) collective-permute-start(bf16[2,2,2,2,16,2064]{5,4,0,1,2,3:T(8,128)(2,1)S(1)} %fusion.7), channel_id=1, source_target_pairs={{0,16},{16,0},{32,48},{48,32},{64,80},{80,64},{96,112},{112,96},{1... | collective-permute-start | bytes 3170312 | tf_op jit(solution)/shard_map/ppermute | solution.py:30
  247.6 1.4 copy-start.2
  249.1 15.8 %collective-permute-start.1 = (bf16[2,2,2,16,2064]{4,3,0,1,2:T(8,128)(2,1)S(1)}, bf16[2,2,2,16,2064]{4,3,0,1,2:T(8,128)(2,1)S(1)}, u32[]{:S(2)}, u32[]{:S(2)}) collective-permute-start(bf16[2,2,2,16,2064]{4,3,0,1,2:T(8,128)(2,1)S(1)} %fusion.8), channel_id=1, source_target_pairs={{0,32},{16,48},{32,0},{48,16},{64,96},{80,112},{96,64},{112,80},{1... | collective-permute-start | bytes 1585160 | tf_op jit(solution)/shard_map/ppermute | solution.py:30
  266.3 10.5 %collective-permute-start.2 = (bf16[2,2,16,2064]{3,2,0,1:T(8,128)(2,1)S(1)}, bf16[2,2,16,2064]{3,2,0,1:T(8,128)(2,1)S(1)}, u32[]{:S(2)}, u32[]{:S(2)}) collective-permute-start(bf16[2,2,16,2064]{3,2,0,1:T(8,128)(2,1)S(1)} %fusion.14), channel_id=1, source_target_pairs={{0,64},{16,80},{32,96},{48,112},{64,0},{80,16},{96,32},{112,48},{1... | collective-permute-start | bytes 792584 | tf_op jit(solution)/shard_map/ppermute | solution.py:30
  276.9 16.3 %collective-permute-start.3 = (bf16[2,16,2064]{2,1,0:T(8,128)(2,1)S(1)}, bf16[2,16,2064]{2,1,0:T(8,128)(2,1)S(1)}, u32[]{:S(2)}, u32[]{:S(2)}) collective-permute-start(bf16[2,16,2064]{2,1,0:T(8,128)(2,1)S(1)} %fusion.16), channel_id=1, source_target_pairs={{0,128},{16,144},{32,160},{48,176},{64,192},{80,208},{96,224},{112... | collective-permute-start | bytes 396296 | tf_op jit(solution)/shard_map/ppermute | solution.py:30
  293.2 0.7 copy-start.5
  294.5 14.4 %collective-permute-start.4 = (bf16[16,2064]{1,0:T(8,128)(2,1)}, bf16[16,2064]{1,0:T(8,128)(2,1)}, u32[]{:S(2)}, u32[]{:S(2)}) collective-permute-start(bf16[16,2064]{1,0:T(8,128)(2,1)} %fusion.22), channel_id=1, source_target_pairs={{0,256},{16,272},{32,288},{48,304},{64,320},{80,336},{96,352},{112... | collective-permute-start | bytes 198152 | tf_op jit(solution)/shard_map/ppermute | solution.py:30
Sparse Core Ops, SparseCore 0:
  13.6 83.8 all-gather.7
  102.1 115.9 all-gather.5

commit v4 on v3

--- a/solution.py
+++ b/solution.py
@@ -29,6 +29,29 @@
         perm = [(i, i ^ (1 << b)) for i in range(axis_n)]
         got = lax.ppermute(send.astype(jnp.bfloat16), axis_name, perm)
         acc = keep + got.astype(jnp.float32)
+    return acc
+
+
+def all_gather_rows(x, axis_name, axis_n):
+    bits = axis_n.bit_length() - 1
+    me = lax.axis_index(axis_name)
+    acc = x
+    for k, b in enumerate(reversed(range(bits))):
+        mine = (me >> b) & 1
+        perm = [(i, i ^ (1 << b)) for i in range(axis_n)]
+        got = lax.ppermute(acc, axis_name, perm)
+        lo = jnp.where(mine == 0, acc, got)
+        hi = jnp.where(mine == 0, got, acc)
+        acc = jnp.stack([lo, hi], axis=k)
+    return acc.reshape((axis_n * x.shape[0],) + x.shape[1:])
+
+
+def all_reduce_sum(x, axis_name, axis_n):
+    bits = axis_n.bit_length() - 1
+    acc = x
+    for b in range(bits):
+        perm = [(i, i ^ (1 << b)) for i in range(axis_n)]
+        acc = acc + lax.ppermute(acc, axis_name, perm)
     return acc
 
 
@@ -103,24 +126,26 @@
     scale = lax.rsqrt(jnp.mean(residual_float * residual_float, axis=-1, keepdims=True) + 1e-06)
     normalized_input = (residual_float * scale * norm_gain.astype(jnp.float32)).astype(jnp.bfloat16)
 
+    piece = all_gather_rows(normalized_input, "tensor", tensor_n)
+
+    db_rows = sel_db.reshape(-1, d_model)
+    db_all = lax.all_gather(db_rows, "tensor", axis=0, tiled=False).reshape(
+        tensor_n, used_n * rank_n, col_n
+    )
+
     def feat_major(a):
         return jnp.transpose(a, (1, 0, 2)).reshape(feat_loc, used_n * rank_n)
 
-    a_rows = jnp.concatenate([feat_major(sel_ga), feat_major(sel_ua)], axis=1).reshape(-1, d_model)
-    db_rows = sel_db.reshape(-1, d_model)
-    tpack = jnp.concatenate([normalized_input, a_rows, db_rows], axis=0)
-    tall = lax.all_gather(tpack, "tensor", axis=0, tiled=False)
-    r0 = tok_dev
-    r1 = r0 + a_rows.shape[0]
-    piece = tall[:, :r0].reshape(group_tok, d_model)
-    both_in = tall[:, r0:r1].reshape(tensor_n * feat_loc, 2 * used_n * rank_n)
-    db_all = tall[:, r1:].reshape(tensor_n, used_n * rank_n, col_n)
-
-    low = jnp.dot(piece, both_in, preferred_element_type=jnp.float32).reshape(
+    both_in = jnp.concatenate([feat_major(sel_ga), feat_major(sel_ua)], axis=1)
+    feat_first = lax.axis_index("tensor") * feat_loc
+    own_cols = lax.dynamic_slice_in_dim(piece, feat_first, feat_loc, 1)
+    low = jnp.dot(own_cols, both_in, preferred_element_type=jnp.float32).reshape(
         group_tok, 2, used_n, rank_n
     )
-    mid_gate = select_token(low[:, 0], token_weights).astype(jnp.bfloat16)
-    mid_up = select_token(low[:, 1], token_weights).astype(jnp.bfloat16)
+    partial_mid = jnp.sum(low * token_weights[:, None, :, None], axis=2)
+    mids = all_reduce_sum(partial_mid, "tensor", tensor_n)
+    mid_gate = mids[:, 0].astype(jnp.bfloat16)
+    mid_up = mids[:, 1].astype(jnp.bfloat16)
     weights_bf = token_weights.astype(jnp.bfloat16)
 
     def spread(mid):

time: 320 us -> 319 us (level)
  waiting for transfers between devices: 230 us -> 138 us
  starting transfers between devices: 16.4 us -> 104 us
  other arithmetic: 9.81 us -> 15.5 us
  local copies, waits for them, and re-layouts: 36.9 us -> 31.9 us
    all_gather x1, waiting for transfers between devices: 111 us -> 37.7 us  [local(): lax.all_gather(db_rows, 'tensor', axis=0, tiled=False)]
    ppermute x0 -> x10, starting transfers between devices: none -> 73.3 us  [the longest x5 39.2 us: all_reduce_sum(): acc = acc + lax.ppermute(acc, axis_name, perm)]
    all_gather x1, waiting for transfers between devices: 80.5 us -> 42.4 us  [local(): whole = lax.all_gather(pack, 'seq', axis=0, tiled=False)]
    ppermute x0 -> x10, waiting for transfers between devices: none -> 28.1 us  [the longest x5 24.5 us: all_gather_rows(): got = lax.ppermute(acc, axis_name, perm)]
    ppermute x5, starting transfers between devices: 16.4 us -> 30.4 us  [reduce_scatter_rows(): got = lax.ppermute(send.astype(jnp.bfloat16), axis_name, perm)]
    ppermute x5, waiting for transfers between devices: 37.8 us -> 29.3 us  [reduce_scatter_rows(): got = lax.ppermute(send.astype(jnp.bfloat16), axis_name, perm)]
    slice x2 -> x0, local copies, waits for them, and re-layouts: 7.16 us -> none  [the longest x1 4.82 us: local(): both_in = tall[:, r0:r1].reshape(tensor_n * feat_loc, 2 * used_n * rank_n)]
    another operation x1 -> x12, other arithmetic: 0.18 us -> 3.6 us  [the longest x10 2.56 us: all_gather_rows(): acc = jnp.stack([lo, hi], axis=k)]
  transfers between devices with their start and end apart: 7 -> 17, of which waited for: 7 -> 14; matrix products, arithmetic and copies ran while one was open for 5% -> 8% of each run, Pallas kernels for 0% -> 0%
where the time goes in v4:
time: 319 us; the launch traced here: 317 us
  waiting for transfers between devices  138 us (43%)
  starting transfers between devices  104 us (33%)
  local copies, waits for them, and re-layouts  31.9 us (10%)
  other arithmetic  15.5 us (5%)
  matrix products  14.6 us (5%)
  between operations  14 us (4%)
    all_gather x1, waiting for transfers between devices, local(): whole = lax.all_gather(pack, 'seq', axis=0, tiled=False)  42.4 us
    ppermute x5, starting transfers between devices, all_reduce_sum(): acc = acc + lax.ppermute(acc, axis_name, perm)  39.2 us
    all_gather x1, waiting for transfers between devices, local(): lax.all_gather(db_rows, 'tensor', axis=0, tiled=False)  37.7 us
    ppermute x5, starting transfers between devices, all_gather_rows(): got = lax.ppermute(acc, axis_name, perm)  34.1 us
    ppermute x5, starting transfers between devices, reduce_scatter_rows(): got = lax.ppermute(send.astype(jnp.bfloat16), axis_name, perm)  30.4 us
    ppermute x5, waiting for transfers between devices, reduce_scatter_rows(): got = lax.ppermute(send.astype(jnp.bfloat16), axis_name, perm)  29.3 us
    ppermute x5, waiting for transfers between devices, all_gather_rows(): got = lax.ppermute(acc, axis_name, perm)  24.5 us
    unnamed x31, local copies, waits for them, and re-layouts  7.7 us
  transfers between devices with their start and end apart: 17, of which 14 were waited for; matrix products, arithmetic and copies ran while one was open for 8% of the time, Pallas kernels for 0%

profile of v4, /device:TPU:1, one launch (start us, length us, event | category | flops | bytes accessed | tf_op | source)
XLA Modules:
  0.0 317.4 jit_solution(5182359873405809787)
XLA Ops:
  9.2 16.3 %collective-permute-start = (bf16[16,2048]{1,0:T(8,128)(2,1)S(1)}, bf16[16,2048]{1,0:T(8,128)(2,1)S(1)}, u32[]{:S(2)}, u32[]{:S(2)}) collective-permute-start(bf16[16,2048]{1,0:T(8,128)(2,1)S(1)} %fusion.15), channel_id=1, source_target_pairs={{0,256},{16,272},{32,288},{48,304},{64,320},{80,336},{96,352},{112... | collective-permute-start | bytes 196616 | tf_op jit(solution)/shard_map/ppermute | solution.py:42
  28.3 5.3 %collective-permute-start.1 = (bf16[2,16,2048]{2,1,0:T(8,128)(2,1)S(1)}, bf16[2,16,2048]{2,1,0:T(8,128)(2,1)S(1)}, u32[]{:S(2)}, u32[]{:S(2)}) collective-permute-start(bf16[2,16,2048]{2,1,0:T(8,128)(2,1)S(1)} %pad_maximum_fusion.4), channel_id=1, source_target_pairs={{0,128},{16,144},{32,160},{48,176},{64,192},{80,208},{96,224},{112... | collective-permute-start | bytes 393224 | tf_op jit(solution)/shard_map/ppermute | solution.py:42
  40.5 6.6 %collective-permute-done.1 = bf16[2,16,2048]{2,1,0:T(8,128)(2,1)S(1)} collective-permute-done((bf16[2,16,2048]{2,1,0:T(8,128)(2,1)S(1)}, bf16[2,16,2048]{2,1,0:T(8,128)(2,1)S(1)}, u32[]{:S(2)}, u32[]{:S(2)}) %collective-permute-start.1) | collective-permute-done | bytes 131104 | tf_op jit(solution)/shard_map/ppermute | solution.py:42
  47.2 4.7 %collective-permute-start.2 = (bf16[2,2,16,2048]{3,2,0,1:T(8,128)(2,1)S(1)}, bf16[2,2,16,2048]{3,2,0,1:T(8,128)(2,1)S(1)}, u32[]{:S(2)}, u32[]{:S(2)}) collective-permute-start(bf16[2,2,16,2048]{3,2,0,1:T(8,128)(2,1)S(1)} %pad_maximum_fusion.3), channel_id=1, source_target_pairs={{0,64},{16,80},{32,96},{48,112},{64,0},{80,16},{96,32},{112,48},{1... | collective-permute-start | bytes 786440 | tf_op jit(solution)/shard_map/ppermute | solution.py:42
  51.9 5.3 %collective-permute-done.2 = bf16[2,2,16,2048]{3,2,0,1:T(8,128)(2,1)S(1)} collective-permute-done((bf16[2,2,16,2048]{3,2,0,1:T(8,128)(2,1)S(1)}, bf16[2,2,16,2048]{3,2,0,1:T(8,128)(2,1)S(1)}, u32[]{:S(2)}, u32[]{:S(2)}) %collective-permute-start.2) | collective-permute-done | bytes 262176 | tf_op jit(solution)/shard_map/ppermute | solution.py:42
  57.2 3.1 collective-permute-start.3
  60.4 10.1 %collective-permute-done.3 = bf16[2,2,2,16,2048]{4,3,0,1,2:T(8,128)(2,1)S(1)} collective-permute-done((bf16[2,2,2,16,2048]{4,3,0,1,2:T(8,128)(2,1)S(1)}, bf16[2,2,2,16,2048]{4,3,0,1,2:T(8,128)(2,1)S(1)}, u32[]{:S(2)}, u32[]{:S(2)}) %collective-permute-start.3) | collective-permute-done | bytes 524320 | tf_op jit(solution)/shard_map/ppermute | solution.py:42
  71.6 4.8 %collective-permute-start.4 = (bf16[2,2,2,2,16,2048]{5,4,0,1,2,3:T(8,128)(2,1)}, bf16[2,2,2,2,16,2048]{5,4,0,1,2,3:T(8,128)(2,1)S(1)}, u32[]{:S(2)}, u32[]{:S(2)}) collective-permute-start(bf16[2,2,2,2,16,2048]{5,4,0,1,2,3:T(8,128)(2,1)} %pad_maximum_fusion.1), channel_id=1, source_target_pairs={{0,16},{16,0},{32,48},{48,32},{64,80},{80,64},{96,112},{112,96},{1... | collective-permute-start | bytes 3145736 | tf_op jit(solution)/shard_map/ppermute | solution.py:42
  79.5 42.4 %all-gather.7.cloned.1.call-done = bf16[16,4,19488]{2,1,0:T(4,128)(2,1)} async-done(((bf16[1,4,19488]{2,1,0:T(4,128)(2,1)}), bf16[16,4,19488]{2,1,0:T(4,128)(2,1)}) %all-gather.7.cloned.1.call-update) | async-done | bytes 2494480 | tf_op jit(solution)/shard_map/all_gather | solution.py:98
  134.4 12.5 %collective-permute-start.5 = (f32[512,2,16]{0,2,1:T(8,128)S(1)}, f32[512,2,16]{0,2,1:T(8,128)S(1)}, u32[]{:S(2)}, u32[]{:S(2)}) collective-permute-start(f32[512,2,16]{0,2,1:T(8,128)S(1)} %multiply_reduce_fusion), channel_id=1, source_target_pairs={{0,16},{16,0},{32,48},{48,32},{64,80},{80,64},{96,112},{112,96},{1... | collective-permute-start | bytes 196616 | tf_op jit(solution)/shard_map/ppermute | solution.py:54
  148.4 3.2 %collective-permute-start.6 = (f32[512,2,16]{0,2,1:T(8,128)}, f32[512,2,16]{0,2,1:T(8,128)}, u32[]{:S(2)}, u32[]{:S(2)}) collective-permute-start(f32[512,2,16]{0,2,1:T(8,128)} %add.107), channel_id=1, source_target_pairs={{0,32},{16,48},{32,0},{48,16},{64,96},{80,112},{96,64},{112,80},{1... | collective-permute-start | bytes 196616 | tf_op jit(solution)/shard_map/ppermute | solution.py:54
  154.6 4.8 %collective-permute-start.7 = (f32[512,2,16]{0,2,1:T(8,128)S(1)}, f32[512,2,16]{0,2,1:T(8,128)S(1)}, u32[]{:S(2)}, u32[]{:S(2)}) collective-permute-start(f32[512,2,16]{0,2,1:T(8,128)S(1)} %add.108), channel_id=1, source_target_pairs={{0,64},{16,80},{32,96},{48,112},{64,0},{80,16},{96,32},{112,48},{1... | collective-permute-start | bytes 196616 | tf_op jit(solution)/shard_map/ppermute | solution.py:54
  159.5 3.2 %fusion.34 = f32[512,342]{0,1:T(8,128)} fusion(bf16[512,2048]{1,0:T(8,128)(2,1)S(1)} %bitcast.102, bf16[2048,342]{0,1:T(8,128)(2,1)} %param.17), kind=kOutput, calls=%fused_computation.88 | convolution fusion | flops 717225984 | bytes 4198400 | tf_op jit(solution)/shard_map/dot_general | solution.py:154
  162.7 7.7 %collective-permute-start.8 = (f32[512,2,16]{0,2,1:T(8,128)S(1)}, f32[512,2,16]{0,2,1:T(8,128)S(1)}, u32[]{:S(2)}, u32[]{:S(2)}) collective-permute-start(f32[512,2,16]{0,2,1:T(8,128)S(1)} %add.109), channel_id=1, source_target_pairs={{0,128},{16,144},{32,160},{48,176},{64,192},{80,208},{96,224},{112... | collective-permute-start | bytes 196616 | tf_op jit(solution)/shard_map/ppermute | solution.py:54
  172.3 10.9 %collective-permute-start.9 = (f32[512,2,16]{0,2,1:T(8,128)S(1)}, f32[512,2,16]{0,2,1:T(8,128)}, u32[]{:S(2)}, u32[]{:S(2)}) collective-permute-start(f32[512,2,16]{0,2,1:T(8,128)S(1)} %add.110), channel_id=1, source_target_pairs={{0,256},{16,272},{32,288},{48,304},{64,320},{80,336},{96,352},{112... | collective-permute-start | bytes 196616 | tf_op jit(solution)/shard_map/ppermute | solution.py:54
  197.3 5.4 %collective-permute-start.10 = (bf16[2,2,2,2,16,2064]{5,4,0,1,2,3:T(8,128)(2,1)S(1)}, bf16[2,2,2,2,16,2064]{5,4,0,1,2,3:T(8,128)(2,1)}, u32[]{:S(2)}, u32[]{:S(2)}) collective-permute-start(bf16[2,2,2,2,16,2064]{5,4,0,1,2,3:T(8,128)(2,1)S(1)} %fusion.7), channel_id=1, source_target_pairs={{0,16},{16,0},{32,48},{48,32},{64,80},{80,64},{96,112},{112,96},{1... | collective-permute-start | bytes 3170312 | tf_op jit(solution)/shard_map/ppermute | solution.py:30
  211.2 13.4 %collective-permute-done.11 = bf16[2,2,2,16,2064]{4,3,0,1,2:T(8,128)(2,1)S(1)} collective-permute-done((bf16[2,2,2,16,2064]{4,3,0,1,2:T(8,128)(2,1)S(1)}, bf16[2,2,2,16,2064]{4,3,0,1,2:T(8,128)(2,1)S(1)}, u32[]{:S(2)}, u32[]{:S(2)}) %collective-permute-start.11) | collective-permute-done | bytes 528416 | tf_op jit(solution)/shard_map/ppermute | solution.py:30
  226.0 5.0 %collective-permute-start.12 = (bf16[2,2,16,2064]{3,2,0,1:T(8,128)(2,1)S(1)}, bf16[2,2,16,2064]{3,2,0,1:T(8,128)(2,1)S(1)}, u32[]{:S(2)}, u32[]{:S(2)}) collective-permute-start(bf16[2,2,16,2064]{3,2,0,1:T(8,128)(2,1)S(1)} %fusion.10), channel_id=1, source_target_pairs={{0,64},{16,80},{32,96},{48,112},{64,0},{80,16},{96,32},{112,48},{1... | collective-permute-start | bytes 792584 | tf_op jit(solution)/shard_map/ppermute | solution.py:30
  231.6 4.9 %collective-permute-done.12 = bf16[2,2,16,2064]{3,2,0,1:T(8,128)(2,1)S(1)} collective-permute-done((bf16[2,2,16,2064]{3,2,0,1:T(8,128)(2,1)S(1)}, bf16[2,2,16,2064]{3,2,0,1:T(8,128)(2,1)S(1)}, u32[]{:S(2)}, u32[]{:S(2)}) %collective-permute-start.12) | collective-permute-done | bytes 264224 | tf_op jit(solution)/shard_map/ppermute | solution.py:30
  236.6 7.1 %collective-permute-start.13 = (bf16[2,16,2064]{2,1,0:T(8,128)(2,1)S(1)}, bf16[2,16,2064]{2,1,0:T(8,128)(2,1)S(1)}, u32[]{:S(2)}, u32[]{:S(2)}) collective-permute-start(bf16[2,16,2064]{2,1,0:T(8,128)(2,1)S(1)} %fusion.12), channel_id=1, source_target_pairs={{0,128},{16,144},{32,160},{48,176},{64,192},{80,208},{96,224},{112... | collective-permute-start | bytes 396296 | tf_op jit(solution)/shard_map/ppermute | solution.py:30
  243.8 8.4 %collective-permute-done.13 = bf16[2,16,2064]{2,1,0:T(8,128)(2,1)S(1)} collective-permute-done((bf16[2,16,2064]{2,1,0:T(8,128)(2,1)S(1)}, bf16[2,16,2064]{2,1,0:T(8,128)(2,1)S(1)}, u32[]{:S(2)}, u32[]{:S(2)}) %collective-permute-start.13) | collective-permute-done | bytes 132128 | tf_op jit(solution)/shard_map/ppermute | solution.py:30
  253.6 10.6 %collective-permute-start.14 = (bf16[16,2064]{1,0:T(8,128)(2,1)}, bf16[16,2064]{1,0:T(8,128)(2,1)}, u32[]{:S(2)}, u32[]{:S(2)}) collective-permute-start(bf16[16,2064]{1,0:T(8,128)(2,1)} %fusion.23), channel_id=1, source_target_pairs={{0,256},{16,272},{32,288},{48,304},{64,320},{80,336},{96,352},{112... | collective-permute-start | bytes 198152 | tf_op jit(solution)/shard_map/ppermute | solution.py:30
  264.4 37.7 %all-gather.5.cloned.1.call-done = bf16[32,8,2048]{2,1,0:T(8,128)(2,1)} async-done(((bf16[1,8,2048]{2,1,0:T(8,128)(2,1)}), bf16[32,8,2048]{2,1,0:T(8,128)(2,1)}) %all-gather.5.cloned.1.call-update) | async-done | bytes 1048592 | tf_op jit(solution)/shard_map/all_gather | solution.py:132
  302.1 3.3 %reshape.229 = bf16[32,256,64]{2,1,0:T(8,128)(2,1)S(1)} reshape(bf16[32,8,2048]{2,1,0:T(8,128)(2,1)} %all-gather.5.cloned.1.call-done) | data formatting | bytes 2097152 | tf_op jit(solution)/shard_map/reshape | solution.py:132
  (120 shorter events, 66.6 us)
Async XLA Ops:
  6.5 183.0 %copy-start = (bf16[342,2048]{1,0:T(8,128)(2,1)S(1)}, bf16[342,2048]{1,0:T(8,128)(2,1)}, u32[]{:S(2)}) copy-start(bf16[342,2048]{1,0:T(8,128)(2,1)} %param.19) | copy-start | bytes 4202500
  6.5 115.4 %all-gather.7.cloned.1.call-start = ((), (), s32[]{:S(2)}) async-start(), calls=%async_computation.1 | async-start | bytes 2663424 | tf_op jit(solution)/shard_map/all_gather | solution.py:98
  9.2 18.1 %collective-permute-start = (bf16[16,2048]{1,0:T(8,128)(2,1)S(1)}, bf16[16,2048]{1,0:T(8,128)(2,1)S(1)}, u32[]{:S(2)}, u32[]{:S(2)}) collective-permute-start(bf16[16,2048]{1,0:T(8,128)(2,1)S(1)} %fusion.15), channel_id=1, source_target_pairs={{0,256},{16,272},{32,288},{48,304},{64,320},{80,336},{96,352},{112... | collective-permute-start | bytes 196616 | tf_op jit(solution)/shard_map/ppermute | solution.py:42
  28.3 18.8 %collective-permute-start.1 = (bf16[2,16,2048]{2,1,0:T(8,128)(2,1)S(1)}, bf16[2,16,2048]{2,1,0:T(8,128)(2,1)S(1)}, u32[]{:S(2)}, u32[]{:S(2)}) collective-permute-start(bf16[2,16,2048]{2,1,0:T(8,128)(2,1)S(1)} %pad_maximum_fusion.4), channel_id=1, source_target_pairs={{0,128},{16,144},{32,160},{48,176},{64,192},{80,208},{96,224},{112... | collective-permute-start | bytes 393224 | tf_op jit(solution)/shard_map/ppermute | solution.py:42
  40.5 261.6 %all-gather.5.cloned.1.call-start = ((), (), s32[]{:S(2)}) async-start(), calls=%async_computation | async-start | bytes 1081344 | tf_op jit(solution)/shard_map/all_gather | solution.py:132
  47.2 9.9 %collective-permute-start.2 = (bf16[2,2,16,2048]{3,2,0,1:T(8,128)(2,1)S(1)}, bf16[2,2,16,2048]{3,2,0,1:T(8,128)(2,1)S(1)}, u32[]{:S(2)}, u32[]{:S(2)}) collective-permute-start(bf16[2,2,16,2048]{3,2,0,1:T(8,128)(2,1)S(1)} %pad_maximum_fusion.3), channel_id=1, source_target_pairs={{0,64},{16,80},{32,96},{48,112},{64,0},{80,16},{96,32},{112,48},{1... | collective-permute-start | bytes 786440 | tf_op jit(solution)/shard_map/ppermute | solution.py:42
  57.2 13.3 %collective-permute-start.3 = (bf16[2,2,2,16,2048]{4,3,0,1,2:T(8,128)(2,1)S(1)}, bf16[2,2,2,16,2048]{4,3,0,1,2:T(8,128)(2,1)S(1)}, u32[]{:S(2)}, u32[]{:S(2)}) collective-permute-start(bf16[2,2,2,16,2048]{4,3,0,1,2:T(8,128)(2,1)S(1)} %pad_maximum_fusion.2), channel_id=1, source_target_pairs={{0,32},{16,48},{32,0},{48,16},{64,96},{80,112},{96,64},{112,80},{1... | collective-permute-start | bytes 1572872 | tf_op jit(solution)/shard_map/ppermute | solution.py:42
  60.4 16.1 %copy-start.10 = (s32[1,8]{1,0:T(1,128)S(1)}, s32[1,8]{1,0:T(1,128)}, u32[]{:S(2)}) copy-start(s32[1,8]{1,0:T(1,128)} %param.26) | copy-start | bytes 100
  60.4 17.0 %copy-start.11 = (s32[64]{0:T(128)S(1)}, s32[64]{0:T(128)}, u32[]{:S(2)}) copy-start(s32[64]{0:T(128)} %param.29) | copy-start | bytes 772
  60.4 17.0 %copy-start.12 = (s32[16]{0:T(128)S(1)}, s32[16]{0:T(128)}, u32[]{:S(2)}) copy-start(s32[16]{0:T(128)} %param.28) | copy-start | bytes 196
  60.4 17.7 %copy-start.8 = (s32[1,8]{1,0:T(1,128)S(1)}, s32[1,8]{1,0:T(1,128)}, u32[]{:S(2)}) copy-start(s32[1,8]{1,0:T(1,128)} %param.27) | copy-start | bytes 100
  71.6 7.3 %collective-permute-start.4 = (bf16[2,2,2,2,16,2048]{5,4,0,1,2,3:T(8,128)(2,1)}, bf16[2,2,2,2,16,2048]{5,4,0,1,2,3:T(8,128)(2,1)S(1)}, u32[]{:S(2)}, u32[]{:S(2)}) collective-permute-start(bf16[2,2,2,2,16,2048]{5,4,0,1,2,3:T(8,128)(2,1)} %pad_maximum_fusion.1), channel_id=1, source_target_pairs={{0,16},{16,0},{32,48},{48,32},{64,80},{80,64},{96,112},{112,96},{1... | collective-permute-start | bytes 3145736 | tf_op jit(solution)/shard_map/ppermute | solution.py:42
  134.4 13.4 %collective-permute-start.5 = (f32[512,2,16]{0,2,1:T(8,128)S(1)}, f32[512,2,16]{0,2,1:T(8,128)S(1)}, u32[]{:S(2)}, u32[]{:S(2)}) collective-permute-start(f32[512,2,16]{0,2,1:T(8,128)S(1)} %multiply_reduce_fusion), channel_id=1, source_target_pairs={{0,16},{16,0},{32,48},{48,32},{64,80},{80,64},{96,112},{112,96},{1... | collective-permute-start | bytes 196616 | tf_op jit(solution)/shard_map/ppermute | solution.py:54
  148.4 5.3 %collective-permute-start.6 = (f32[512,2,16]{0,2,1:T(8,128)}, f32[512,2,16]{0,2,1:T(8,128)}, u32[]{:S(2)}, u32[]{:S(2)}) collective-permute-start(f32[512,2,16]{0,2,1:T(8,128)} %add.107), channel_id=1, source_target_pairs={{0,32},{16,48},{32,0},{48,16},{64,96},{80,112},{96,64},{112,80},{1... | collective-permute-start | bytes 196616 | tf_op jit(solution)/shard_map/ppermute | solution.py:54
  154.6 8.0 %collective-permute-start.7 = (f32[512,2,16]{0,2,1:T(8,128)S(1)}, f32[512,2,16]{0,2,1:T(8,128)S(1)}, u32[]{:S(2)}, u32[]{:S(2)}) collective-permute-start(f32[512,2,16]{0,2,1:T(8,128)S(1)} %add.108), channel_id=1, source_target_pairs={{0,64},{16,80},{32,96},{48,112},{64,0},{80,16},{96,32},{112,48},{1... | collective-permute-start | bytes 196616 | tf_op jit(solution)/shard_map/ppermute | solution.py:54
  162.7 20.5 %copy-start.5 = (bf16[16,19488]{1,0:T(8,128)(2,1)S(1)}, bf16[16,19488]{1,0:T(8,128)(2,1)}, u32[]{:S(2)}) copy-start(bf16[16,19488]{1,0:T(8,128)(2,1)} %copy-done.4) | copy-start | bytes 1870852
  162.7 9.6 %collective-permute-start.8 = (f32[512,2,16]{0,2,1:T(8,128)S(1)}, f32[512,2,16]{0,2,1:T(8,128)S(1)}, u32[]{:S(2)}, u32[]{:S(2)}) collective-permute-start(f32[512,2,16]{0,2,1:T(8,128)S(1)} %add.109), channel_id=1, source_target_pairs={{0,128},{16,144},{32,160},{48,176},{64,192},{80,208},{96,224},{112... | collective-permute-start | bytes 196616 | tf_op jit(solution)/shard_map/ppermute | solution.py:54
  172.3 14.6 %collective-permute-start.9 = (f32[512,2,16]{0,2,1:T(8,128)S(1)}, f32[512,2,16]{0,2,1:T(8,128)}, u32[]{:S(2)}, u32[]{:S(2)}) collective-permute-start(f32[512,2,16]{0,2,1:T(8,128)S(1)} %add.110), channel_id=1, source_target_pairs={{0,256},{16,272},{32,288},{48,304},{64,320},{80,336},{96,352},{112... | collective-permute-start | bytes 196616 | tf_op jit(solution)/shard_map/ppermute | solution.py:54
  197.3 7.9 %collective-permute-start.10 = (bf16[2,2,2,2,16,2064]{5,4,0,1,2,3:T(8,128)(2,1)S(1)}, bf16[2,2,2,2,16,2064]{5,4,0,1,2,3:T(8,128)(2,1)}, u32[]{:S(2)}, u32[]{:S(2)}) collective-permute-start(bf16[2,2,2,2,16,2064]{5,4,0,1,2,3:T(8,128)(2,1)S(1)} %fusion.7), channel_id=1, source_target_pairs={{0,16},{16,0},{32,48},{48,32},{64,80},{80,64},{96,112},{112,96},{1... | collective-permute-start | bytes 3170312 | tf_op jit(solution)/shard_map/ppermute | solution.py:30
  208.8 22.1 %copy-start.7 = (bf16[16,1024]{1,0:T(8,128)(2,1)S(1)}, bf16[16,1024]{1,0:T(8,128)(2,1)}, u32[]{:S(2)}) copy-start(bf16[16,1024]{1,0:T(8,128)(2,1)} %get-tuple-element.9) | copy-start | bytes 98308
  208.9 15.7 %collective-permute-start.11 = (bf16[2,2,2,16,2064]{4,3,0,1,2:T(8,128)(2,1)S(1)}, bf16[2,2,2,16,2064]{4,3,0,1,2:T(8,128)(2,1)S(1)}, u32[]{:S(2)}, u32[]{:S(2)}) collective-permute-start(bf16[2,2,2,16,2064]{4,3,0,1,2:T(8,128)(2,1)S(1)} %fusion.8), channel_id=1, source_target_pairs={{0,32},{16,48},{32,0},{48,16},{64,96},{80,112},{96,64},{112,80},{1... | collective-permute-start | bytes 1585160 | tf_op jit(solution)/shard_map/ppermute | solution.py:30
  226.0 10.6 %collective-permute-start.12 = (bf16[2,2,16,2064]{3,2,0,1:T(8,128)(2,1)S(1)}, bf16[2,2,16,2064]{3,2,0,1:T(8,128)(2,1)S(1)}, u32[]{:S(2)}, u32[]{:S(2)}) collective-permute-start(bf16[2,2,16,2064]{3,2,0,1:T(8,128)(2,1)S(1)} %fusion.10), channel_id=1, source_target_pairs={{0,64},{16,80},{32,96},{48,112},{64,0},{80,16},{96,32},{112,48},{1... | collective-permute-start | bytes 792584 | tf_op jit(solution)/shard_map/ppermute | solution.py:30
  236.6 15.6 %collective-permute-start.13 = (bf16[2,16,2064]{2,1,0:T(8,128)(2,1)S(1)}, bf16[2,16,2064]{2,1,0:T(8,128)(2,1)S(1)}, u32[]{:S(2)}, u32[]{:S(2)}) collective-permute-start(bf16[2,16,2064]{2,1,0:T(8,128)(2,1)S(1)} %fusion.12), channel_id=1, source_target_pairs={{0,128},{16,144},{32,160},{48,176},{64,192},{80,208},{96,224},{112... | collective-permute-start | bytes 396296 | tf_op jit(solution)/shard_map/ppermute | solution.py:30
  253.6 53.5 %collective-permute-start.14 = (bf16[16,2064]{1,0:T(8,128)(2,1)}, bf16[16,2064]{1,0:T(8,128)(2,1)}, u32[]{:S(2)}, u32[]{:S(2)}) collective-permute-start(bf16[16,2064]{1,0:T(8,128)(2,1)} %fusion.23), channel_id=1, source_target_pairs={{0,256},{16,272},{32,288},{48,304},{64,320},{80,336},{96,352},{112... | collective-permute-start | bytes 198152 | tf_op jit(solution)/shard_map/ppermute | solution.py:30
  (7 other events, 25.0 us)
Sparse Core Ops, SparseCore 0:
  40.6 81.2 all-gather.6
  231.7 70.3 all-gather.4
